TPU v7x, 32 devices: a whole 2x2x4 slice. The times are simulated.
32 devices in a mesh: dp: 8 (over z, y), tensor: 4 (over x, core).
Axes of the slice: x: 2, y: 2, z: 4, core: 2. Of those that a mesh axis runs over, the one named last changes fastest.
Arguments:
- tokens: bfloat16 [8, 1024, 1536], P('dp'), may hold values from -6 to 6
- piece_starts: int32 [8, 2], P('dp'), may hold values from -1 to 768, as said below
- attn_gain: bfloat16 [1536], P('dp'), may hold values from 0.5 to 1.5
- w_query: bfloat16 [1536, 1536], P('dp', 'tensor'), may hold values from -0.15625 to 0.15625
- w_key: bfloat16 [1536, 1536], P('dp', 'tensor'), may hold values from -0.15625 to 0.15625
- w_value: bfloat16 [1536, 1536], P('dp', 'tensor'), may hold values from -0.15625 to 0.15625
- w_outgate: bfloat16 [1536, 1536], P('dp', 'tensor'), may hold values from -0.15625 to 0.15625
- w_forget: bfloat16 [1536, 24], P('dp', 'tensor'), may hold values from -0.3125 to 0.3125
- forget_bias: float32 [24], P('tensor'), may hold values from 2 to 8
- w_output: bfloat16 [1536, 1536], P('tensor', 'dp'), may hold values from -0.4375 to 0.4375
- ffn_gain: bfloat16 [1536], P('dp'), may hold values from 0.5 to 1.5
- w_gate: bfloat16 [1536, 4096], P('dp', 'tensor'), may hold values from -0.15625 to 0.15625
- w_up: bfloat16 [1536, 4096], P('dp', 'tensor'), may hold values from -0.15625 to 0.15625
- w_down: bfloat16 [4096, 1536], P('tensor', 'dp'), may hold values from -0.09375 to 0.09375
- cotangent: bfloat16 [8, 1024, 1536], P('dp'), may hold values from -6 to 6
Outputs:
- output: bfloat16 [8, 1024, 1536], P('dp')
- tokens_grad: bfloat16 [8, 1024, 1536], P('dp')
- attn_gain_grad: float32 [1536], P('dp')
- w_query_grad: float32 [1536, 1536], P('dp', 'tensor')
- w_key_grad: float32 [1536, 1536], P('dp', 'tensor')
- w_value_grad: float32 [1536, 1536], P('dp', 'tensor')
- w_outgate_grad: float32 [1536, 1536], P('dp', 'tensor')
- w_forget_grad: float32 [1536, 24], P('dp', 'tensor')
- forget_bias_grad: float32 [24], P('tensor')
- w_output_grad: float32 [1536, 1536], P('tensor', 'dp')
- ffn_gain_grad: float32 [1536], P('dp')
- w_gate_grad: float32 [1536, 4096], P('dp', 'tensor')
- w_up_grad: float32 [1536, 4096], P('dp', 'tensor')
- w_down_grad: float32 [4096, 1536], P('tensor', 'dp')
Inputs may be any that keep to these rules, and one draw needn't show every extreme that they name: `piece_starts`: slot k of a sequence's row holds -1 (no piece) or a start in [k * 512, (k + 1) * 512 - 256], so pieces never intersect; the number of pieces differs between sequences.
All inputs are finite; a program needn't handle non-finite values.
Results may differ from a plain program's by a relative error of at most 0.025.
Values may be sent and summed in bfloat16 or wider, within the bound.
No kernel may reach another device: no remote copies, remote signals or barrier semaphores. Data moves between devices by JAX's collectives and lax.ppermute only.
A program may use at most 256 MiB of HBM per device.

v0:
```python
import jax
import jax.numpy as jnp
from jax import lax
from jax.sharding import PartitionSpec as P

PIECE = 256
epsilon = 1e-06
masked_value = -1e30


def project(left, right):
    return jnp.dot(left, right, preferred_element_type=jnp.float32)


def contract_rows(left, right):
    return lax.dot_general(
        left, right, (((0,), (0,)), ((), ())), preferred_element_type=jnp.float32
    )


def contract_cols(left, right):
    return lax.dot_general(
        left, right, (((1,), (1,)), ((), ())), preferred_element_type=jnp.float32
    )


def allowed_pairs(starts, length):
    places = jnp.arange(length, dtype=jnp.int32)
    inside = (
        (starts[:, None] >= 0)
        & (places[None, :] >= starts[:, None])
        & (places[None, :] < starts[:, None] + PIECE)
    )
    labels = jnp.sum(
        jnp.where(inside, jnp.arange(1, starts.shape[0] + 1, dtype=jnp.int32)[:, None], 0), axis=0
    )
    same = (labels[:, None] == labels[None, :]) & (labels[:, None] > 0)
    return (places[None, :] <= places[:, None]) | same


def block_scores(query_rows, key_all, decay, allowed_rows, first_row):
    count = query_rows.shape[0]
    raw = jnp.einsum(
        "qhd,khd->hqk", query_rows, key_all, preferred_element_type=jnp.float32
    ) * query_rows.shape[-1] ** (-0.5)
    apart = (
        lax.slice_in_dim(decay, first_row, first_row + count, axis=1)[:, :, None]
        - decay[:, None, :]
    )
    return (jnp.where(allowed_rows[None], raw - jnp.abs(apart), masked_value), apart)


def attend_forward(items):
    query_all, key_all, value_all, log_forget, starts = items
    length = query_all.shape[0]
    block_rows = min(512, length)
    decay = jnp.cumsum(log_forget, axis=0).T
    allowed = allowed_pairs(starts, length)
    results = []
    normalizers = []
    for first_row in range(0, length, block_rows):
        scores, apart = block_scores(
            query_all[first_row : first_row + block_rows],
            key_all,
            decay,
            allowed[first_row : first_row + block_rows],
            first_row,
        )
        largest = jnp.max(scores, axis=-1, keepdims=True)
        weights = jnp.exp(scores - largest)
        denominator = jnp.sum(weights, axis=-1, keepdims=True)
        chances = (weights / denominator).astype(jnp.bfloat16)
        results.append(
            jnp.einsum("hqk,khd->qhd", chances, value_all, preferred_element_type=jnp.float32)
        )
        normalizers.append(largest + jnp.log(denominator))
    return (jnp.concatenate(results, axis=0), jnp.concatenate(normalizers, axis=1))


def attend_backward(items):
    query_all, key_all, value_all, log_forget, starts, attended, normalizer, grad_out = items
    length = query_all.shape[0]
    block_rows = min(512, length)
    scale = query_all.shape[-1] ** (-0.5)
    decay = jnp.cumsum(log_forget, axis=0).T
    allowed = allowed_pairs(starts, length)
    grad_key = jnp.zeros(key_all.shape, jnp.float32)
    grad_value = jnp.zeros(value_all.shape, jnp.float32)
    grad_decay = jnp.zeros(decay.shape, jnp.float32)
    query_parts = []
    row_parts = []
    for first_row in range(0, length, block_rows):
        query_rows = query_all[first_row : first_row + block_rows]
        out_rows = grad_out[first_row : first_row + block_rows]
        scores, apart = block_scores(
            query_rows, key_all, decay, allowed[first_row : first_row + block_rows], first_row
        )
        chances = jnp.exp(scores - normalizer[:, first_row : first_row + block_rows])
        grad_chance = jnp.einsum(
            "qhd,khd->hqk", out_rows, value_all, preferred_element_type=jnp.float32
        )
        offset = jnp.sum(
            out_rows.astype(jnp.float32) * attended[first_row : first_row + block_rows], axis=-1
        ).T[:, :, None]
        grad_score = chances * (grad_chance - offset)
        grad_rounded = grad_score.astype(jnp.bfloat16)
        grad_value = grad_value + jnp.einsum(
            "hqk,qhd->khd",
            chances.astype(jnp.bfloat16),
            out_rows,
            preferred_element_type=jnp.float32,
        )
        grad_key = (
            grad_key
            + jnp.einsum(
                "hqk,qhd->khd", grad_rounded, query_rows, preferred_element_type=jnp.float32
            )
            * scale
        )
        query_parts.append(
            jnp.einsum("hqk,khd->qhd", grad_rounded, key_all, preferred_element_type=jnp.float32)
            * scale
        )
        signed = grad_score * jnp.sign(apart)
        grad_decay = grad_decay + jnp.sum(signed, axis=1)
        row_parts.append(-jnp.sum(signed, axis=-1))
    grad_decay = grad_decay + jnp.concatenate(row_parts, axis=1)
    grad_log = jnp.flip(jnp.cumsum(jnp.flip(grad_decay, axis=1), axis=1), axis=1).T
    grad_query = jnp.concatenate(query_parts, axis=0)
    return (
        grad_query.astype(jnp.bfloat16),
        grad_key.astype(jnp.bfloat16),
        grad_value.astype(jnp.bfloat16),
        grad_log,
    )


def on_device(
    tokens,
    piece_starts,
    attn_gain,
    w_query,
    w_key,
    w_value,
    w_outgate,
    w_forget,
    forget_bias,
    w_output,
    ffn_gain,
    w_gate,
    w_up,
    w_down,
    cotangent,
):
    sequences, length, width = tokens.shape
    heads_here = w_forget.shape[1]
    share_width = w_query.shape[1]
    head_size = share_width // heads_here
    row_count = sequences * length
    block = w_query.shape[0]
    units = w_gate.shape[1]

    def head_view(values):
        return values.reshape(sequences, length, heads_here, head_size)

    attn_local = jnp.concatenate(
        [w_query, w_key, w_value, w_outgate, w_output.T, w_forget, attn_gain[:, None]], axis=1
    )
    attn_full = lax.all_gather(attn_local, "dp", axis=0, tiled=True)
    joined = attn_full[:, : 4 * share_width]
    output_t = attn_full[:, 4 * share_width : 5 * share_width]
    forget_w = attn_full[:, 5 * share_width : 5 * share_width + heads_here]
    gain_one = attn_full[:, 5 * share_width + heads_here].astype(jnp.float32)
    ffn_local = jnp.concatenate([w_gate, w_up, w_down.T, ffn_gain[:, None]], axis=1)
    ffn_full = lax.all_gather(ffn_local, "dp", axis=0, tiled=True)
    gate_up_w = ffn_full[:, : 2 * units]
    down_t = ffn_full[:, 2 * units : 3 * units]
    gain_two = ffn_full[:, 3 * units].astype(jnp.float32)
    inputs = tokens.reshape(row_count, width).astype(jnp.float32)
    scale_one = lax.rsqrt(jnp.mean(inputs * inputs, axis=-1, keepdims=True) + epsilon)
    unit_one = inputs * scale_one
    normed = (unit_one * gain_one).astype(jnp.bfloat16)
    projected = project(normed, joined)
    query_all = head_view(projected[:, :share_width].astype(jnp.bfloat16))
    key_all = head_view(projected[:, share_width : 2 * share_width].astype(jnp.bfloat16))
    value_all = head_view(projected[:, 2 * share_width : 3 * share_width].astype(jnp.bfloat16))
    gate_pre = projected[:, 3 * share_width :]
    forget_pre = project(normed, forget_w) + forget_bias[None, :]
    log_forget = jax.nn.log_sigmoid(forget_pre).reshape(sequences, length, heads_here)
    attended, normalizer = lax.map(
        attend_forward, (query_all, key_all, value_all, log_forget, piece_starts)
    )
    attended_flat = attended.reshape(row_count, share_width)
    gate_open = jax.nn.sigmoid(gate_pre)
    gated = (attended_flat * gate_open).astype(jnp.bfloat16)
    attention = lax.psum(contract_cols(gated, output_t).astype(jnp.bfloat16), "tensor").astype(
        jnp.float32
    )
    hidden = inputs + attention
    scale_two = lax.rsqrt(jnp.mean(hidden * hidden, axis=-1, keepdims=True) + epsilon)
    unit_two = hidden * scale_two
    normed_two = (unit_two * gain_two).astype(jnp.bfloat16)
    inner_pre = project(normed_two, gate_up_w)
    gate_part = inner_pre[:, :units]
    up_part = inner_pre[:, units:]
    inner = (jax.nn.silu(gate_part) * up_part).astype(jnp.bfloat16)
    ffn_out = lax.psum(contract_cols(inner, down_t).astype(jnp.bfloat16), "tensor").astype(
        jnp.float32
    )
    output = (hidden + ffn_out).astype(jnp.bfloat16).reshape(tokens.shape)
    upstream_low = cotangent.reshape(row_count, width)
    upstream = upstream_low.astype(jnp.float32)
    grad_down_t = contract_rows(upstream_low, inner)
    grad_inner = project(upstream_low, down_t)
    sigma = jax.nn.sigmoid(gate_part)
    grad_gate = (grad_inner * up_part * sigma * (1.0 + gate_part * (1.0 - sigma))).astype(
        jnp.bfloat16
    )
    grad_up = (grad_inner * gate_part * sigma).astype(jnp.bfloat16)
    grad_gate_up = jnp.concatenate([grad_gate, grad_up], axis=1)
    grad_gate_up_w = contract_rows(normed_two, grad_gate_up)
    grad_normed_two = lax.psum(
        contract_cols(grad_gate_up, gate_up_w).astype(jnp.bfloat16), "tensor"
    ).astype(jnp.float32)
    grad_ffn_gain = jnp.sum(grad_normed_two * unit_two, axis=0)
    ffn_sums = lax.psum_scatter(
        jnp.concatenate([grad_gate_up_w, grad_down_t, grad_ffn_gain[:, None]], axis=1).astype(
            jnp.bfloat16
        ),
        "dp",
        scatter_dimension=0,
        tiled=True,
    ).astype(jnp.float32)
    grad_unit_two = grad_normed_two * gain_two
    grad_hidden = upstream + scale_two * (
        grad_unit_two - unit_two * jnp.mean(grad_unit_two * unit_two, axis=-1, keepdims=True)
    )
    hidden_low = grad_hidden.astype(jnp.bfloat16)
    grad_output_t = contract_rows(hidden_low, gated)
    grad_gated = project(hidden_low, output_t)
    grad_attended = (grad_gated * gate_open).astype(jnp.bfloat16)
    grad_gate_pre = (grad_gated * attended_flat * gate_open * (1.0 - gate_open)).astype(
        jnp.bfloat16
    )
    grad_query, grad_key, grad_value, grad_log = lax.map(
        attend_backward,
        (
            query_all,
            key_all,
            value_all,
            log_forget,
            piece_starts,
            attended,
            normalizer,
            head_view(grad_attended),
        ),
    )
    grad_forget = (grad_log.reshape(row_count, heads_here) * jax.nn.sigmoid(-forget_pre)).astype(
        jnp.bfloat16
    )
    grad_four = jnp.concatenate(
        [
            grad_query.reshape(row_count, share_width),
            grad_key.reshape(row_count, share_width),
            grad_value.reshape(row_count, share_width),
            grad_gate_pre,
        ],
        axis=1,
    )
    grad_joined = contract_rows(normed, grad_four)
    grad_forget_w = contract_rows(normed, grad_forget)
    grad_bias = jnp.sum(grad_forget.astype(jnp.float32), axis=0)
    grad_normed = lax.psum(
        (contract_cols(grad_four, joined) + contract_cols(grad_forget, forget_w)).astype(
            jnp.bfloat16
        ),
        "tensor",
    ).astype(jnp.float32)
    grad_attn_gain = jnp.sum(grad_normed * unit_one, axis=0)
    grad_unit_one = grad_normed * gain_one
    grad_inputs = grad_hidden + scale_one * (
        grad_unit_one - unit_one * jnp.mean(grad_unit_one * unit_one, axis=-1, keepdims=True)
    )
    tokens_grad = grad_inputs.astype(jnp.bfloat16).reshape(tokens.shape)
    place = jnp.arange(width, dtype=jnp.int32) % block
    bias_col = jnp.where(
        place < heads_here, jnp.take(grad_bias, jnp.minimum(place, heads_here - 1)), 0.0
    )
    attn_sums = lax.psum_scatter(
        jnp.concatenate(
            [grad_joined, grad_output_t, grad_forget_w, grad_attn_gain[:, None], bias_col[:, None]],
            axis=1,
        ).astype(jnp.bfloat16),
        "dp",
        scatter_dimension=0,
        tiled=True,
    ).astype(jnp.float32)
    forget_at = 5 * share_width
    return (
        output,
        tokens_grad,
        attn_sums[:, forget_at + heads_here],
        attn_sums[:, :share_width],
        attn_sums[:, share_width : 2 * share_width],
        attn_sums[:, 2 * share_width : 3 * share_width],
        attn_sums[:, 3 * share_width : 4 * share_width],
        attn_sums[:, forget_at : forget_at + heads_here],
        attn_sums[:heads_here, forget_at + heads_here + 1],
        attn_sums[:, 4 * share_width : 5 * share_width].T,
        ffn_sums[:, 3 * units],
        ffn_sums[:, :units],
        ffn_sums[:, units : 2 * units],
        ffn_sums[:, 2 * units : 3 * units].T,
    )


def solution(mesh):
    placed = (
        P("dp", None, None),
        P("dp", None),
        P("dp"),
        P("dp", "tensor"),
        P("dp", "tensor"),
        P("dp", "tensor"),
        P("dp", "tensor"),
        P("dp", "tensor"),
        P("tensor"),
        P("tensor", "dp"),
        P("dp"),
        P("dp", "tensor"),
        P("dp", "tensor"),
        P("tensor", "dp"),
        P("dp", None, None),
    )
    return jax.shard_map(
        on_device,
        mesh=mesh,
        in_specs=placed,
        out_specs=(
            P("dp", None, None),
            P("dp", None, None),
            P("dp"),
            P("dp", "tensor"),
            P("dp", "tensor"),
            P("dp", "tensor"),
            P("dp", "tensor"),
            P("dp", "tensor"),
            P("tensor"),
            P("tensor", "dp"),
            P("dp"),
            P("dp", "tensor"),
            P("dp", "tensor"),
            P("tensor", "dp"),
        ),
        check_vma=False,
    )
```

profile of v0, /device:TPU:0, one launch (start us, length us, event | category | flops | bytes accessed | tf_op | source)
XLA Modules:
  0.0 1067.8 jit_solution(12600640613263816599)
XLA Ops:
  9.0 2.1 concatenate.40
  13.2 2.6 fusion.31
  18.3 94.3 %all-gather.3.cloned.1.call-done = bf16[1536,1927]{1,0:T(8,128)(2,1)} async-done(((bf16[192,1927]{1,0:T(8,128)(2,1)}), bf16[1536,1927]{1,0:T(8,128)(2,1)}) %all-gather.3.cloned.1.call-update) | async-done | bytes 5919760 | tf_op jit(solution)/shard_map/all_gather | solution.py:169
  113.9 9.4 fusion.126
  125.6 2.3 copy.114
  127.9 2.0 convolution_add_fusion
  134.5 2.4 copy.116
  136.9 1.9 copy.115
  138.9 5.2 fusion.127
  144.1 2.8 fusion.7
  148.6 4.3 fusion.84
  152.9 4.0 fusion.128
  156.9 2.8 fusion.6
  159.7 1.7 copy-done
  161.6 3.8 fusion.85
  166.9 3.1 copy.118
  170.0 2.3 multiply_convert_fusion.5
  173.2 4.8 convolution_convert_fusion.2
  178.8 2.2 pad_maximum_fusion.6
  181.1 63.7 %all-reduce.5.cloned.1.call-done = bf16[1024,1536]{1,0:T(8,128)(2,1)} async-done(((bf16[1024,1536]{1,0:T(8,128)(2,1)}), bf16[1024,1536]{1,0:T(8,128)(2,1)}) %all-reduce.5.cloned.1.call-update) | async-done | bytes 3145744 | tf_op jit(solution)/shard_map/psum | solution.py:196
  244.8 3.0 multiply_reduce_fusion
  247.8 142.1 %all-gather.5.cloned.1.call-done = bf16[1536,3073]{1,0:T(8,128)(2,1)} async-done(((bf16[192,3073]{1,0:T(8,128)(2,1)}), bf16[1536,3073]{1,0:T(8,128)(2,1)}) %all-gather.5.cloned.1.call-update) | async-done | bytes 9440272 | tf_op jit(solution)/shard_map/all_gather | solution.py:175
  391.1 12.1 %fusion.43 = f32[1024,2048]{1,0:T(8,128)} fusion(bf16[1536,3073]{1,0:T(8,128)(2,1)} %all-gather.5.cloned.1.call-done, bf16[1024,1536]{1,0:T(8,128)(2,1)} %all-reduce.5.cloned.1.call-done, bf16[1,1024,1536]{2,1,0:T(8,128)(2,1)S(1)} %copy-done.1, f32[1536]{0:T(1024)S(1)} %convert_reduce_fusion, f32[1024]{0:T(1024)S(1)} %add_rsqrt_fusion), kind=kOutput, calls=%fused_computation.66 | convolution fusion | flops 6451888128 | bytes 20981760 | tf_op jit(solution)/shard_map/dot_general | solution.py:12
  403.2 8.5 fusion.47
  413.7 8.0 fusion.55
  422.5 7.6 convolution_convert_fusion.4
  430.1 58.4 %all-reduce.7.cloned.1.call-done = bf16[1024,1536]{1,0:T(8,128)(2,1)} async-done(((bf16[1024,1536]{1,0:T(8,128)(2,1)}), bf16[1024,1536]{1,0:T(8,128)(2,1)}) %all-reduce.7.cloned.1.call-update) | async-done | bytes 3145744 | tf_op jit(solution)/shard_map/psum | solution.py:222
  488.6 6.1 fusion.27
  494.7 2.6 fusion.26
  497.3 6.9 multiply_convert_fusion.4
  506.4 2.0 multiply_reduce_fusion.1
  508.4 7.0 fusion.32
  517.8 9.2 subtract_multiply_fusion.1
  527.1 17.0 %fusion.11 = (f32[6,1024]{1,0:T(8,128)}, f32[6,512]{1,0:T(8,128)}, f32[6,512]{1,0:T(8,128)}, f32[6,1024]{1,0:T(8,128)}, bf16[6,512,1024]{2,1,0:T(8,128)(2,1)S(1)}) fusion(f32[6,512]{1,0:T(8,128)} %get-tuple-element.169, f32[6,1024]{1,0:T(8,128)S(1)} %bitcast.188, f32[6,512,1024]{2,1,0:T(8,128)} %subtract_multiply_fusion.1, ...), kind=kOutput, calls=%fused_computation.23 | convolution fusion | flops 446674944 | bytes 32784384 | tf_op jit(solution)/shard_map/while/body/eval_jaxpr/qhd,khd->hqk/dot_general | solution.py:99
  544.1 2.4 fusion.64
  546.5 2.8 fusion.92
  549.2 7.5 fusion.95
  556.8 3.1 add_convert_fusion.2
  559.9 2.3 copy.129
  562.2 7.2 multiply_convert_fusion.3
  569.5 2.3 copy.128
  576.1 4.2 rev.9
  581.6 4.1 reduce-window.16
  588.2 4.2 rev.10
  593.3 9.0 fusion.51
  602.4 3.7 add_convert_fusion
  607.0 4.5 fusion.110
  611.5 2.2 convolution_convert_fusion.6
  613.8 5.4 convolution_convert_fusion.5
  619.2 9.9 convolution_convert_fusion
  629.1 97.0 %all-reduce.9.cloned.1.call-done = (bf16[1024,1536]{1,0:T(8,128)(2,1)}, bf16[1024,1536]{1,0:T(8,128)(2,1)}) async-done(((bf16[1024,1536]{1,0:T(8,128)(2,1)}, bf16[1024,1536]{1,0:T(8,128)(2,1)}), (bf16[1024,1536]{1,0:T(8,128)(2,1)}, bf16[1024,1536]{1,0:T(8,128)(2,1)})) %all-reduce.9.cloned.1.call-update) | async-done | bytes 6291472 | tf_op jit(solution)/shard_map/psum | solution.py:207
  726.0 3.8 fusion.30
  729.9 26.6 %concatenate.49 = bf16[1536,1928]{0,1:T(8,128)(2,1)} concatenate(bf16[1536,1536]{0,1:T(8,128)(2,1)} %convolution_convert_fusion, bf16[1536,384]{0,1:T(8,128)(2,1)} %convolution_convert_fusion.5, bf16[1536,6]{0,1:T(8,128)(2,1)S(1)} %copy-done.51, bf16[1536,1]{0,1:T(2,128)(2,1)S(1)} %broadcast_in_dim.195, bf16[1536,1]{0,1:T(2,128)(2,1)S(1)} %copy-done.52), dimensions={1} | concatenate | bytes 11845632 | tf_op jit(solution)/shard_map/concatenate | solution.py:290
  756.4 8.7 copy.140
  765.4 6.1 fusion.58
  771.6 7.9 convolution_convert_fusion.1
  779.8 4.9 pad_maximum_fusion
  784.7 8.8 fusion.60
  793.6 89.9 %reduce-scatter.7.cloned.1.call-done = bf16[192,1928]{1,0:T(8,128)(2,1)} async-done(((bf16[1536,1928]{1,0:T(8,128)(2,1)}), bf16[192,1928]{1,0:T(8,128)(2,1)}) %reduce-scatter.7.cloned.1.call-update) | async-done | bytes 740368
  883.5 1.8 copy.141
  887.6 1.9 copy.132
  889.5 1.9 copy.133
  891.4 1.9 copy.134
  895.5 160.7 %reduce-scatter.5.cloned.1.call-done = bf16[192,3073]{1,0:T(8,128)(2,1)} async-done(((bf16[1536,3073]{1,0:T(8,128)(2,1)}), bf16[192,3073]{1,0:T(8,128)(2,1)}) %reduce-scatter.5.cloned.1.call-update) | async-done | bytes 1180048 | tf_op jit(solution)/shard_map/reduce_scatter | solution.py:226
  (205 shorter events, 47.7 us)
Async XLA Ops:
  7.2 106.8 %copy-start.1 = (bf16[1,1024,1536]{2,1,0:T(8,128)(2,1)S(1)}, bf16[1,1024,1536]{2,1,0:T(8,128)(2,1)}, u32[]{:S(2)}) copy-start(bf16[1,1024,1536]{2,1,0:T(8,128)(2,1)} %param.15) | copy-start | bytes 9437188
  7.2 105.4 %all-gather.3.cloned.1.call-start = ((), (), s32[]{:S(2)}) async-start(), calls=%async_computation.2 | async-start | bytes 7077888 | tf_op jit(solution)/shard_map/all_gather | solution.py:169
  11.1 233.7 %all-reduce.5.cloned.1.call-start = ((), (), s32[]{:S(2)}) async-start(), calls=%async_computation.3 | async-start | bytes 6291456 | tf_op jit(solution)/shard_map/psum | solution.py:196
  15.8 112.2 %copy-start.49 = (f32[1024]{0:T(1024)}, f32[1024]{0:T(1024)S(1)}, u32[]{:S(2)}) copy-start(f32[1024]{0:T(1024)S(1)} %add_rsqrt_fusion.1) | copy-start | bytes 12292
  113.9 14.0 %copy-start.35 = (f32[1536]{0:T(1024)}, f32[1536]{0:T(1024)S(1)}, u32[]{:S(2)}) copy-start(f32[1536]{0:T(1024)S(1)} %convert_reduce_fusion.1) | copy-start | bytes 18436
  123.4 4.6 copy-start.57
  134.5 9.5 copy-start.22
  144.1 4.5 copy-start.3
  144.1 4.5 copy-start.14
  146.9 6.0 copy-start.39
  148.5 4.3 copy-start.7
  148.5 4.4 copy-start.25
  148.5 4.4 copy-start.28
  148.5 4.4 copy-start.32
  148.6 4.4 copy-start.55
  152.9 12.6 %copy-start.16 = (f32[512,6,64]{0,2,1:T(8,128)}, f32[512,6,64]{0,2,1:T(8,128)S(1)}, u32[]{:S(2)}) copy-start(f32[512,6,64]{0,2,1:T(8,128)S(1)} %fusion.84) | copy-start | bytes 2359300
  156.9 4.5 copy-start
  156.9 4.7 copy-start.41
  161.6 3.8 copy-start.43
  173.2 5.6 copy-start.29
  178.0 211.9 %all-gather.5.cloned.1.call-start = ((), (), s32[]{:S(2)}) async-start(), calls=%async_computation.4 | async-start | bytes 11059200 | tf_op jit(solution)/shard_map/all_gather | solution.py:175
  181.1 307.5 %all-reduce.7.cloned.1.call-start = ((), (), s32[]{:S(2)}) async-start(), calls=%async_computation.5 | async-start | bytes 6291456 | tf_op jit(solution)/shard_map/psum | solution.py:222
  247.8 246.9 %copy-start.47 = (f32[1024]{0:T(1024)}, f32[1024]{0:T(1024)S(1)}, u32[]{:S(2)}) copy-start(f32[1024]{0:T(1024)S(1)} %add_rsqrt_fusion) | copy-start | bytes 12292
  391.1 103.6 %copy-start.37 = (f32[1536]{0:T(1024)}, f32[1536]{0:T(1024)S(1)}, u32[]{:S(2)}) copy-start(f32[1536]{0:T(1024)S(1)} %convert_reduce_fusion) | copy-start | bytes 18436
  391.1 12.1 %copy-start.20 = (bf16[1,1024,1536]{2,1,0:T(8,128)(2,1)S(1)}, bf16[1,1024,1536]{2,1,0:T(8,128)(2,1)}, u32[]{:S(2)}) copy-start(bf16[1,1024,1536]{2,1,0:T(8,128)(2,1)} %param.29) | copy-start | bytes 9437188
  391.1 12.1 %copy-start.56 = (bf16[1536,3073]{1,0:T(8,128)(2,1)S(1)}, bf16[1536,3073]{1,0:T(8,128)(2,1)}, u32[]{:S(2)}) copy-start(bf16[1536,3073]{1,0:T(8,128)(2,1)} %all-gather.5.cloned.1.call-done) | copy-start | bytes 28320772
  413.7 8.1 copy-start.40
  413.7 8.8 copy-start.42
  413.7 8.8 copy-start.44
  421.8 304.3 %all-reduce.9.cloned.1.call-start = ((), (), s32[]{:S(2)}) async-start(), calls=%async_computation.8 | async-start | bytes 12582912 | tf_op jit(solution)/shard_map/psum | solution.py:207
  488.6 6.1 copy-start.4
  488.6 6.1 copy-start.6
  488.6 6.1 copy-start.21
  497.3 6.9 copy-start.2
  506.3 9.0 copy-start.12
  517.7 9.3 copy-start.13
  517.8 9.3 copy-start.15
  517.8 9.3 copy-start.33
  517.8 9.3 copy-start.46
  527.1 17.0 %copy-start.23 = (bf16[512,384]{0,1:T(8,128)(2,1)S(1)}, bf16[512,384]{0,1:T(8,128)(2,1)}, u32[]{:S(2)}) copy-start(bf16[512,384]{0,1:T(8,128)(2,1)} %copy-done.22) | copy-start | bytes 1179652
  544.1 12.7 %slice-start = ((s8[12582912]{0:T(1024)(128)(4,1)}), s8[4194304]{0:T(1024)(128)(4,1)S(1)}, s32[]{:S(2)}) async-start(s8[12582912]{0:T(1024)(128)(4,1)} %bitcast.158), calls=%async_computation.9 | async-start | bytes 8388608
  544.1 12.7 %slice-start.1 = ((s8[12582912]{0:T(1024)(128)(4,1)}), s8[4194304]{0:T(1024)(128)(4,1)S(1)}, s32[]{:S(2)}) async-start(s8[12582912]{0:T(1024)(128)(4,1)} %bitcast.158), calls=%async_computation.10 | async-start | bytes 8388608
  549.2 7.5 slice-start.2
  549.2 7.5 copy-start.11
  562.2 9.6 copy-start.24
  562.2 12.4 %copy-start.54 = (f32[6,512]{1,0:T(8,128)S(1)}, f32[6,512]{1,0:T(8,128)}, u32[]{:S(2)}) copy-start(f32[6,512]{1,0:T(8,128)} %get-tuple-element.141) | copy-start | bytes 36868
  593.3 9.0 copy-start.45
  602.4 9.1 copy-start.36
  602.4 9.1 copy-start.50
  606.1 277.4 %reduce-scatter.7.cloned.1.call-start = ((), (), s32[]{:S(2)}) async-start(), calls=%async_computation.7 | async-start | bytes 7077888
  606.4 7.4 copy-start.19
  613.7 5.4 copy-start.26
  613.7 5.4 copy-start.27
  613.7 5.4 copy-start.30
  613.7 5.4 copy-start.58
  629.1 100.8 %copy-start.51 = (bf16[1536,6]{0,1:T(8,128)(2,1)S(1)}, bf16[1536,6]{0,1:T(8,128)(2,1)}, u32[]{:S(2)}) copy-start(bf16[1536,6]{0,1:T(8,128)(2,1)} %convolution_convert_fusion.6) | copy-start | bytes 55300
  629.1 100.8 %copy-start.52 = (bf16[1536,1]{0,1:T(2,128)(2,1)S(1)}, bf16[1536,1]{0,1:T(2,128)(2,1)}, u32[]{:S(2)}) copy-start(bf16[1536,1]{0,1:T(2,128)(2,1)} %fusion.110) | copy-start | bytes 9220
  765.1 6.5 copy-start.38
  765.1 6.5 copy-start.48
  765.1 291.0 %reduce-scatter.5.cloned.1.call-start = ((), (), s32[]{:S(2)}) async-start(), calls=%async_computation.6 | async-start | bytes 11059200 | tf_op jit(solution)/shard_map/reduce_scatter | solution.py:226
  765.4 6.2 copy-start.5
  765.4 6.2 copy-start.60
  765.4 6.2 copy-start.62
  771.6 7.9 copy-start.53
  (9 other events, 15.1 us)
Sparse Core Ops, SparseCore 0:
  11.2 101.4 all-gather.2
  178.1 66.6 all-reduce.4
  247.5 142.3 all-gather.4
  421.9 66.5 all-reduce.6
  606.3 119.7 all-reduce.8
  765.2 118.2 reduce-scatter.6
  887.1 168.9 reduce-scatter.4
where the time goes:
time: 1080 us; the launch traced here: 1070 us
  waiting for transfers between devices  706 us (65%)
  matrix products  177 us (16%)
  local copies, waits for them, and re-layouts  99 us (9%)
  other arithmetic  69.5 us (6%)
  between operations  15.2 us (1%)
    reduce_scatter x1, waiting for transfers between devices, on_device(): lax.psum_scatter(jnp.concatenate([grad_gate_up_w, grad_down_t, grad_ffn_g...  161 us
    all_gather x1, waiting for transfers between devices, on_device(): ffn_full = lax.all_gather(ffn_local, 'dp', axis=0, tiled=True)  142 us
    psum x1, waiting for transfers between devices, on_device(): lax.psum(contract_cols(inner, down_t).astype(jnp.bfloat16), 'tensor')  97 us
    all_gather x1, waiting for transfers between devices, on_device(): attn_full = lax.all_gather(attn_local, 'dp', axis=0, tiled=True)  94.3 us
    unnamed x8, waiting for transfers between devices  90.1 us
    psum x1, waiting for transfers between devices, on_device(): lax.psum(contract_cols(gated, output_t).astype(jnp.bfloat16), 'tensor')  63.7 us
    psum x1, waiting for transfers between devices, on_device(): lax.psum(contract_cols(grad_gate_up, gate_up_w).astype(jnp.bfloat16), 'te...  58.4 us
    dot_general x5, matrix products, project(): return jnp.dot(left, right, preferred_element_type=jnp.float32)  39 us
  transfers between devices with their start and end apart: 7, of which 7 were waited for; matrix products, arithmetic and copies ran while one was open for 8% of the time, Pallas kernels for 0%

commit v1 on v0

--- a/solution.py
+++ b/solution.py
@@ -166,7 +166,27 @@
     attn_local = jnp.concatenate(
         [w_query, w_key, w_value, w_outgate, w_output.T, w_forget, attn_gain[:, None]], axis=1
     )
-    attn_full = lax.all_gather(attn_local, "dp", axis=0, tiled=True)
+    top = lax.axis_size("dp")
+    back = lax.axis_index("dp")
+    response, val2, inter = (top, back, attn_local.shape[0])
+    fields = [(src_i, (src_i + 1) % response) for src_i in range(response)]
+    attn_full = jnp.zeros(
+        (*attn_local.shape[:0], response * inter, *attn_local.shape[1:]), attn_local.dtype
+    )
+    attn_full = lax.dynamic_update_slice_in_dim(attn_full, attn_local, val2 * inter, axis=0)
+    cards = [(src_i, (src_i - 1) % response) for src_i in range(response)]
+    heard = response // 2
+    later = a_next = attn_local
+    for b in range(1, heard + 1):
+        later = lax.ppermute(later, "dp", fields)
+        attn_full = lax.dynamic_update_slice_in_dim(
+            attn_full, later, (val2 - b) % response * inter, axis=0
+        )
+        if b < response - heard:
+            a_next = lax.ppermute(a_next, "dp", cards)
+            attn_full = lax.dynamic_update_slice_in_dim(
+                attn_full, a_next, (val2 + b) % response * inter, axis=0
+            )
     joined = attn_full[:, : 4 * share_width]
     output_t = attn_full[:, 4 * share_width : 5 * share_width]
     forget_w = attn_full[:, 5 * share_width : 5 * share_width + heads_here]

time: 1080 us -> 1120 us (1.037)
  local copies, waits for them, and re-layouts: 99 us -> 192 us
  waiting for transfers between devices: 706 us -> 627 us
  starting transfers between devices: 0.67 us -> 20.5 us
    all_gather x1 -> x0, waiting for transfers between devices: 94.3 us -> none  [on_device(): attn_full = lax.all_gather(attn_local, 'dp', axis=0, tiled=True)]
    dynamic_update_slice x0 -> x8, local copies, waits for them, and re-layouts: none -> 86.5 us  [the longest x4 42.6 us: on_device(): lax.dynamic_update_slice_in_dim(attn_full, later, (val2 - b) % response *...]
    ppermute x0 -> x7, waiting for transfers between devices: none -> 84.5 us  [the longest x4 84.5 us: on_device(): later = lax.ppermute(later, 'dp', fields)]
    all_gather x1, waiting for transfers between devices: 142 us -> 73.5 us  [on_device(): ffn_full = lax.all_gather(ffn_local, 'dp', axis=0, tiled=True)]
    ppermute x0 -> x7, starting transfers between devices: none -> 19.8 us  [the longest x4 10.6 us: on_device(): later = lax.ppermute(later, 'dp', fields)]
    ppermute x0 -> x7, local copies, waits for them, and re-layouts: none -> 11.3 us  [the longest x4 6.04 us: on_device(): later = lax.ppermute(later, 'dp', fields)]
    unnamed x144 -> x160, local copies, waits for them, and re-layouts: 28 us -> 27 us
    unnamed x8 -> x7, waiting for transfers between devices: 90.1 us -> 89.9 us
  transfers between devices with their start and end apart: 7 -> 13, of which waited for: 7 -> 9; matrix products, arithmetic and copies ran while one was open for 8% -> 16% of each run, Pallas kernels for 0% -> 0%
where the time goes in v1:
time: 1120 us; the launch traced here: 1110 us
  waiting for transfers between devices  627 us (56%)
  local copies, waits for them, and re-layouts  192 us (17%)
  matrix products  183 us (16%)
  other arithmetic  69.6 us (6%)
  starting transfers between devices  20.5 us (2%)
  between operations  16.6 us (1%)
    reduce_scatter x1, waiting for transfers between devices, on_device(): lax.psum_scatter(jnp.concatenate([grad_gate_up_w, grad_down_t, grad_ffn_g...  158 us
    psum x1, waiting for transfers between devices, on_device(): lax.psum(contract_cols(inner, down_t).astype(jnp.bfloat16), 'tensor')  96.5 us
    unnamed x7, waiting for transfers between devices  89.9 us
    ppermute x4, waiting for transfers between devices, on_device(): later = lax.ppermute(later, 'dp', fields)  84.5 us
    all_gather x1, waiting for transfers between devices, on_device(): ffn_full = lax.all_gather(ffn_local, 'dp', axis=0, tiled=True)  73.5 us
    psum x1, waiting for transfers between devices, on_device(): lax.psum(contract_cols(gated, output_t).astype(jnp.bfloat16), 'tensor')  65.7 us
    psum x1, waiting for transfers between devices, on_device(): lax.psum(contract_cols(grad_gate_up, gate_up_w).astype(jnp.bfloat16), 'te...  58.4 us
    dynamic_update_slice x4, local copies, waits for them, and re-layouts, on_device(): lax.dynamic_update_slice_in_dim(attn_full, later, (val2 - b) % response *...  42.6 us
  transfers between devices with their start and end apart: 13, of which 9 were waited for; matrix products, arithmetic and copies ran while one was open for 16% of the time, Pallas kernels for 0%

profile of v1, /device:TPU:0, one launch (start us, length us, event | category | flops | bytes accessed | tf_op | source)
XLA Modules:
  0.0 1108.0 jit_solution(3408065705223934649)
XLA Ops:
  11.0 3.0 collective-permute-start
  14.0 3.1 collective-permute-start.1
  17.1 30.5 %collective-permute-done = bf16[192,1927]{1,0:T(8,128)(2,1)S(1)} collective-permute-done((bf16[192,1927]{1,0:T(8,128)(2,1)S(1)}, bf16[192,1927]{1,0:T(8,128)(2,1)S(1)}, u32[]{:S(2)}, u32[]{:S(2)}) %collective-permute-start) | collective-permute-done | bytes 740000 | tf_op jit(solution)/shard_map/ppermute | solution.py:181
  47.7 2.5 collective-permute-start.2
  50.8 3.0 collective-permute-start.3
  53.8 29.1 %collective-permute-done.2 = bf16[192,1927]{1,0:T(8,128)(2,1)S(1)} collective-permute-done((bf16[192,1927]{1,0:T(8,128)(2,1)S(1)}, bf16[192,1927]{1,0:T(8,128)(2,1)S(1)}, u32[]{:S(2)}, u32[]{:S(2)}) %collective-permute-start.2) | collective-permute-done | bytes 740000 | tf_op jit(solution)/shard_map/ppermute | solution.py:181
  82.9 2.5 collective-permute-start.4
  86.8 2.6 fusion.31
  89.4 3.1 collective-permute-start.5
  92.5 24.9 %collective-permute-done.4 = bf16[192,1927]{1,0:T(8,128)(2,1)} collective-permute-done((bf16[192,1927]{1,0:T(8,128)(2,1)S(1)}, bf16[192,1927]{1,0:T(8,128)(2,1)}, u32[]{:S(2)}, u32[]{:S(2)}) %collective-permute-start.4) | collective-permute-done | bytes 740000 | tf_op jit(solution)/shard_map/ppermute | solution.py:181
  117.4 2.6 collective-permute-start.6
  120.9 2.9 broadcast_in_dim.190
  123.8 10.2 dynamic_update_slice.40
  137.3 10.6 dynamic_update_slice.41
  148.7 11.3 %dynamic_update_slice.42 = bf16[1536,1927]{0,1:T(8,128)(2,1)} dynamic-update-slice(bf16[1536,1927]{0,1:T(8,128)(2,1)} %dynamic_update_slice.41, bf16[192,1927]{0,1:T(8,128)(2,1)S(1)} %copy.132, s32[]{:T(128)S(6)} %select_n.151, s32[]{:T(128)} %constant.170.clone.1) | dynamic-update-slice | bytes 1479940 | tf_op jit(solution)/shard_map/dynamic_update_slice | solution.py:187
  160.9 9.8 dynamic_update_slice.43
  172.9 10.6 dynamic_update_slice.44
  185.7 11.8 %dynamic_update_slice.45 = bf16[1536,1927]{0,1:T(8,128)(2,1)} dynamic-update-slice(bf16[1536,1927]{0,1:T(8,128)(2,1)} %dynamic_update_slice.44, bf16[192,1927]{0,1:T(8,128)(2,1)} %copy.135, s32[]{:T(128)S(6)} %select_n.157, s32[]{:T(128)} %constant.170.clone.1) | dynamic-update-slice | bytes 1479940 | tf_op jit(solution)/shard_map/dynamic_update_slice | solution.py:182
  199.7 11.8 %dynamic_update_slice.46 = bf16[1536,1927]{0,1:T(8,128)(2,1)} dynamic-update-slice(bf16[1536,1927]{0,1:T(8,128)(2,1)} %dynamic_update_slice.45, bf16[192,1927]{0,1:T(8,128)(2,1)} %copy.136, s32[]{:T(128)S(6)} %select_n.159, s32[]{:T(128)} %constant.170.clone.1) | dynamic-update-slice | bytes 1479940 | tf_op jit(solution)/shard_map/dynamic_update_slice | solution.py:187
  213.7 10.4 dynamic_update_slice.47
  224.9 9.5 fusion.127
  238.9 4.5 reduce-window.14
  250.9 2.4 copy.138
  253.4 5.2 fusion.128
  258.6 2.8 fusion.7
  263.1 3.8 fusion.83
  267.0 3.9 fusion.129
  271.0 2.8 fusion.6
  275.7 4.0 fusion.84
  281.1 3.0 copy.142
  287.4 4.8 convolution_convert_fusion.2
  295.3 65.7 %all-reduce.5.cloned.1.call-done = bf16[1024,1536]{1,0:T(8,128)(2,1)} async-done(((bf16[1024,1536]{1,0:T(8,128)(2,1)}), bf16[1024,1536]{1,0:T(8,128)(2,1)}) %all-reduce.5.cloned.1.call-update) | async-done | bytes 3145744 | tf_op jit(solution)/shard_map/psum | solution.py:216
  361.0 3.0 multiply_reduce_fusion
  364.0 73.5 %all-gather.2.cloned.1.call-done = bf16[1536,3073]{1,0:T(8,128)(2,1)} async-done(((bf16[192,3073]{1,0:T(8,128)(2,1)}), bf16[1536,3073]{1,0:T(8,128)(2,1)}) %all-gather.2.cloned.1.call-update) | async-done | bytes 9440272 | tf_op jit(solution)/shard_map/all_gather | solution.py:195
  438.8 12.0 %fusion.43 = f32[1024,2048]{1,0:T(8,128)} fusion(bf16[1536,3073]{1,0:T(8,128)(2,1)} %all-gather.2.cloned.1.call-done, bf16[1024,1536]{1,0:T(8,128)(2,1)} %all-reduce.5.cloned.1.call-done, bf16[1,1024,1536]{2,1,0:T(8,128)(2,1)S(1)} %copy-done.2, f32[1536]{0:T(1024)S(1)} %convert_reduce_fusion, f32[1024]{0:T(1024)S(1)} %add_rsqrt_fusion), kind=kOutput, calls=%fused_computation.66 | convolution fusion | flops 6451888128 | bytes 20981760 | tf_op jit(solution)/shard_map/dot_general | solution.py:12
  450.8 8.5 fusion.47
  461.3 8.0 fusion.54
  470.0 7.6 convolution_convert_fusion.4
  477.7 58.4 %all-reduce.7.cloned.1.call-done = bf16[1024,1536]{1,0:T(8,128)(2,1)} async-done(((bf16[1024,1536]{1,0:T(8,128)(2,1)}), bf16[1024,1536]{1,0:T(8,128)(2,1)}) %all-reduce.7.cloned.1.call-update) | async-done | bytes 3145744 | tf_op jit(solution)/shard_map/psum | solution.py:242
  536.1 5.8 fusion.27
  542.0 2.6 fusion.26
  544.6 6.9 multiply_convert_fusion.2
  558.8 7.9 fusion.32
  566.8 8.9 subtract_multiply_fusion.1
  575.8 18.1 %fusion.11 = (f32[6,1024]{1,0:T(8,128)}, f32[6,512]{1,0:T(8,128)}, f32[6,512]{1,0:T(8,128)}, f32[6,1024]{1,0:T(8,128)}, bf16[6,512,1024]{2,1,0:T(8,128)(2,1)}) fusion(f32[6,512]{1,0:T(8,128)S(1)} %copy-done.62, f32[6,1024]{1,0:T(8,128)S(1)} %bitcast.188, f32[6,512,1024]{2,1,0:T(8,128)} %subtract_multiply_fusion.1, f32[6,512]{1,0:T(8,128)S(1)} %copy-done.61, ...), kind=kOutput, calls=%fused_computation.23 | convolution fusion | flops 446674944 | bytes 32784384 | tf_op jit(solution)/shard_map/while/body/eval_jaxpr/qhd,khd->hqk/dot_general | solution.py:99
  593.9 6.0 fusion.91
  599.9 5.4 fusion.63
  605.3 4.1 fusion.94
  609.4 4.3 add_convert_fusion.2
  622.9 7.2 multiply_convert_fusion.3
  637.2 11.1 %add_convert_fusion = bf16[1024,1536]{1,0:T(8,128)(2,1)} fusion(f32[1024,1536]{1,0:T(8,128)S(1)} %fusion.106, bf16[1536,1927]{0,1:T(8,128)(2,1)} %dynamic_update_slice.47, bf16[1024,384]{1,0:T(8,128)(2,1)S(1)} %copy-done.65, bf16[1024,384]{1,0:T(8,128)(2,1)S(1)} %copy-done.26, bf16[1024,384]{1,0:T(8,128)(2,1)S(1)} %copy-done.28, ...), kind=kOutput, calls=%fused_computation.55 | convolution fusion | flops 4850712576 | bytes 17301504 | tf_op jit(solution)/shard_map/dot_general | solution.py:22
  649.6 4.5 fusion.111
  656.4 5.4 convolution_convert_fusion.5
  661.8 9.9 convolution_convert_fusion
  671.7 96.5 %all-reduce.9.cloned.1.call-done = (bf16[1024,1536]{1,0:T(8,128)(2,1)}, bf16[1024,1536]{1,0:T(8,128)(2,1)}) async-done(((bf16[1024,1536]{1,0:T(8,128)(2,1)}, bf16[1024,1536]{1,0:T(8,128)(2,1)}), (bf16[1024,1536]{1,0:T(8,128)(2,1)}, bf16[1024,1536]{1,0:T(8,128)(2,1)})) %all-reduce.9.cloned.1.call-update) | async-done | bytes 6291472 | tf_op jit(solution)/shard_map/psum | solution.py:227
  768.2 3.8 fusion.30
  772.1 26.6 %concatenate.49 = bf16[1536,1928]{0,1:T(8,128)(2,1)} concatenate(bf16[1536,1536]{0,1:T(8,128)(2,1)} %convolution_convert_fusion, bf16[1536,384]{0,1:T(8,128)(2,1)} %convolution_convert_fusion.5, bf16[1536,6]{0,1:T(8,128)(2,1)S(1)} %copy-done.57, bf16[1536,1]{0,1:T(2,128)(2,1)S(1)} %broadcast_in_dim.199, bf16[1536,1]{0,1:T(2,128)(2,1)S(1)} %copy-done.58), dimensions={1} | concatenate | bytes 11845632 | tf_op jit(solution)/shard_map/concatenate | solution.py:310
  798.7 8.7 copy.164
  807.7 6.1 fusion.57
  813.9 7.9 convolution_convert_fusion.1
  822.0 4.9 pad_maximum_fusion
  827.0 8.8 fusion.59
  835.8 89.8 %reduce-scatter.7.cloned.1.call-done = bf16[192,1928]{1,0:T(8,128)(2,1)} async-done(((bf16[1536,1928]{1,0:T(8,128)(2,1)}), bf16[192,1928]{1,0:T(8,128)(2,1)}) %reduce-scatter.7.cloned.1.call-update) | async-done | bytes 740368
  937.6 158.4 %reduce-scatter.5.cloned.1.call-done = bf16[192,3073]{1,0:T(8,128)(2,1)} async-done(((bf16[1536,3073]{1,0:T(8,128)(2,1)}), bf16[192,3073]{1,0:T(8,128)(2,1)}) %reduce-scatter.5.cloned.1.call-update) | async-done | bytes 1180048 | tf_op jit(solution)/shard_map/reduce_scatter | solution.py:246
  (249 shorter events, 91.7 us)
Async XLA Ops:
  8.0 353.0 %all-reduce.5.cloned.1.call-start = ((), (), s32[]{:S(2)}) async-start(), calls=%async_computation.2 | async-start | bytes 6291456 | tf_op jit(solution)/shard_map/psum | solution.py:216
  11.0 36.7 %collective-permute-start = (bf16[192,1927]{1,0:T(8,128)(2,1)S(1)}, bf16[192,1927]{1,0:T(8,128)(2,1)S(1)}, u32[]{:S(2)}, u32[]{:S(2)}) collective-permute-start(bf16[192,1927]{1,0:T(8,128)(2,1)S(1)} %concatenate.40), channel_id=1, source_target_pairs={{0,4},{4,8},{8,12},{12,16},{16,20},{20,24},{24,28},{28,0},{1,5},{5... | collective-permute-start | bytes 2219912 | tf_op jit(solution)/shard_map/ppermute | solution.py:181
  14.0 36.8 %collective-permute-start.1 = (bf16[192,1927]{1,0:T(8,128)(2,1)S(1)}, bf16[192,1927]{1,0:T(8,128)(2,1)S(1)}, u32[]{:S(2)}, u32[]{:S(2)}) collective-permute-start(bf16[192,1927]{1,0:T(8,128)(2,1)S(1)} %concatenate.40), channel_id=1, source_target_pairs={{0,28},{4,0},{8,4},{12,8},{16,12},{20,16},{24,20},{28,24},{1,29},{... | collective-permute-start | bytes 2219912 | tf_op jit(solution)/shard_map/ppermute | solution.py:186
  47.7 35.3 %copy-start.24 = (bf16[192,1927]{1,0:T(8,128)(2,1)}, bf16[192,1927]{1,0:T(8,128)(2,1)S(1)}, u32[]{:S(2)}) copy-start(bf16[192,1927]{1,0:T(8,128)(2,1)S(1)} %collective-permute-done) | copy-start | bytes 2219908
  47.7 35.3 %collective-permute-start.2 = (bf16[192,1927]{1,0:T(8,128)(2,1)S(1)}, bf16[192,1927]{1,0:T(8,128)(2,1)S(1)}, u32[]{:S(2)}, u32[]{:S(2)}) collective-permute-start(bf16[192,1927]{1,0:T(8,128)(2,1)S(1)} %collective-permute-done), channel_id=1, source_target_pairs={{0,4},{4,8},{8,12},{12,16},{16,20},{20,24},{24,28},{28,0},{1,5},{5... | collective-permute-start | bytes 2219912 | tf_op jit(solution)/shard_map/ppermute | solution.py:181
  50.8 38.6 %collective-permute-start.3 = (bf16[192,1927]{1,0:T(8,128)(2,1)S(1)}, bf16[192,1927]{1,0:T(8,128)(2,1)}, u32[]{:S(2)}, u32[]{:S(2)}) collective-permute-start(bf16[192,1927]{1,0:T(8,128)(2,1)S(1)} %collective-permute-done.1), channel_id=1, source_target_pairs={{0,28},{4,0},{8,4},{12,8},{16,12},{20,16},{24,20},{28,24},{1,29},{... | collective-permute-start | bytes 2219912 | tf_op jit(solution)/shard_map/ppermute | solution.py:186
  82.9 34.5 %collective-permute-start.4 = (bf16[192,1927]{1,0:T(8,128)(2,1)S(1)}, bf16[192,1927]{1,0:T(8,128)(2,1)}, u32[]{:S(2)}, u32[]{:S(2)}) collective-permute-start(bf16[192,1927]{1,0:T(8,128)(2,1)S(1)} %collective-permute-done.2), channel_id=1, source_target_pairs={{0,4},{4,8},{8,12},{12,16},{16,20},{20,24},{24,28},{28,0},{1,5},{5... | collective-permute-start | bytes 2219912 | tf_op jit(solution)/shard_map/ppermute | solution.py:181
  89.4 147.1 %copy-start.54 = (f32[1024]{0:T(1024)}, f32[1024]{0:T(1024)S(1)}, u32[]{:S(2)}) copy-start(f32[1024]{0:T(1024)S(1)} %add_rsqrt_fusion.1) | copy-start | bytes 12292
  89.4 108.1 %collective-permute-start.5 = (bf16[192,1927]{1,0:T(8,128)(2,1)}, bf16[192,1927]{1,0:T(8,128)(2,1)}, u32[]{:S(2)}, u32[]{:S(2)}) collective-permute-start(bf16[192,1927]{1,0:T(8,128)(2,1)} %collective-permute-done.3), channel_id=1, source_target_pairs={{0,28},{4,0},{8,4},{12,8},{16,12},{20,16},{24,20},{28,24},{1,29},{... | collective-permute-start | bytes 2219912 | tf_op jit(solution)/shard_map/ppermute | solution.py:186
  117.4 94.1 %collective-permute-start.6 = (bf16[192,1927]{1,0:T(8,128)(2,1)}, bf16[192,1927]{1,0:T(8,128)(2,1)}, u32[]{:S(2)}, u32[]{:S(2)}) collective-permute-start(bf16[192,1927]{1,0:T(8,128)(2,1)} %collective-permute-done.4), channel_id=1, source_target_pairs={{0,4},{4,8},{8,12},{12,16},{16,20},{20,24},{24,28},{28,0},{1,5},{5... | collective-permute-start | bytes 2219912 | tf_op jit(solution)/shard_map/ppermute | solution.py:181
  120.8 15.6 %copy-start.25 = (bf16[192,1927]{1,0:T(8,128)(2,1)S(1)}, bf16[192,1927]{1,0:T(8,128)(2,1)}, u32[]{:S(2)}) copy-start(bf16[192,1927]{1,0:T(8,128)(2,1)} %copy-done.24) | copy-start | bytes 2219908
  172.9 51.9 %copy-start.2 = (bf16[1,1024,1536]{2,1,0:T(8,128)(2,1)S(1)}, bf16[1,1024,1536]{2,1,0:T(8,128)(2,1)}, u32[]{:S(2)}) copy-start(bf16[1,1024,1536]{2,1,0:T(8,128)(2,1)} %param.15) | copy-start | bytes 9437188
  224.9 11.6 %copy-start.39 = (f32[1536]{0:T(1024)}, f32[1536]{0:T(1024)S(1)}, u32[]{:S(2)}) copy-start(f32[1536]{0:T(1024)S(1)} %fusion.110) | copy-start | bytes 18436
  224.9 11.6 %copy-start.64 = (f32[6]{0:T(128)S(1)}, f32[6]{0:T(128)}, u32[]{:S(2)}) copy-start(f32[6]{0:T(128)} %param.23) | copy-start | bytes 76
  250.9 7.6 copy-start.20
  261.4 5.5 copy-start.44
  267.0 12.7 %copy-start.14 = (f32[512,6,64]{0,2,1:T(8,128)}, f32[512,6,64]{0,2,1:T(8,128)S(1)}, u32[]{:S(2)}) copy-start(f32[512,6,64]{0,2,1:T(8,128)S(1)} %fusion.83) | copy-start | bytes 2359300
  271.0 4.5 copy-start
  271.0 4.7 copy-start.46
  287.4 5.6 copy-start.31
  292.2 145.4 %all-gather.2.cloned.1.call-start = ((), (), s32[]{:S(2)}) async-start(), calls=%async_computation.3 | async-start | bytes 11059200 | tf_op jit(solution)/shard_map/all_gather | solution.py:195
  295.2 240.9 %all-reduce.7.cloned.1.call-start = ((), (), s32[]{:S(2)}) async-start(), calls=%async_computation.4 | async-start | bytes 6291456 | tf_op jit(solution)/shard_map/psum | solution.py:242
  364.0 177.9 %copy-start.52 = (f32[1024]{0:T(1024)}, f32[1024]{0:T(1024)S(1)}, u32[]{:S(2)}) copy-start(f32[1024]{0:T(1024)S(1)} %add_rsqrt_fusion) | copy-start | bytes 12292
  438.8 103.2 %copy-start.41 = (f32[1536]{0:T(1024)}, f32[1536]{0:T(1024)S(1)}, u32[]{:S(2)}) copy-start(f32[1536]{0:T(1024)S(1)} %convert_reduce_fusion) | copy-start | bytes 18436
  438.8 12.0 %copy-start.18 = (bf16[1,1024,1536]{2,1,0:T(8,128)(2,1)S(1)}, bf16[1,1024,1536]{2,1,0:T(8,128)(2,1)}, u32[]{:S(2)}) copy-start(bf16[1,1024,1536]{2,1,0:T(8,128)(2,1)} %param.29) | copy-start | bytes 9437188
  438.8 12.0 %copy-start.63 = (bf16[1536,3073]{1,0:T(8,128)(2,1)S(1)}, bf16[1536,3073]{1,0:T(8,128)(2,1)}, u32[]{:S(2)}) copy-start(bf16[1536,3073]{1,0:T(8,128)(2,1)} %all-gather.2.cloned.1.call-done) | copy-start | bytes 28320772
  461.3 8.1 copy-start.45
  461.3 8.7 copy-start.47
  461.3 8.7 copy-start.49
  469.3 298.9 %all-reduce.9.cloned.1.call-start = ((), (), s32[]{:S(2)}) async-start(), calls=%async_computation.7 | async-start | bytes 12582912 | tf_op jit(solution)/shard_map/psum | solution.py:227
  536.1 5.8 copy-start.5
  536.1 5.8 copy-start.7
  536.1 5.8 copy-start.19
  544.6 7.0 copy-start.3
  558.8 7.9 copy-start.13
  558.8 7.9 copy-start.43
  566.7 9.0 copy-start.11
  566.7 9.0 copy-start.37
  566.8 9.0 copy-start.51
  566.8 9.0 copy-start.61
  566.8 9.0 copy-start.62
  593.9 6.0 copy-start.21
  593.9 11.3 %copy-start.1 = (f32[6,512,1024]{2,1,0:T(8,128)S(1)}, f32[6,512,1024]{2,1,0:T(8,128)}, u32[]{:S(2)}) copy-start(f32[6,512,1024]{2,1,0:T(8,128)} %subtract_multiply_fusion.1) | copy-start | bytes 37748740
  599.9 9.5 slice-start
  599.9 9.5 slice-start.1
  622.9 12.4 %copy-start.50 = (bf16[1024,6]{0,1:T(8,128)(2,1)}, bf16[1024,6]{0,1:T(8,128)(2,1)S(1)}, u32[]{:S(2)}) copy-start(bf16[1024,6]{0,1:T(8,128)(2,1)S(1)} %get-tuple-element.146) | copy-start | bytes 36868
  622.9 11.4 %copy-start.22 = (bf16[6,64,512]{2,1,0:T(8,128)(2,1)S(1)}, bf16[6,64,512]{2,1,0:T(8,128)(2,1)}, u32[]{:S(2)}) copy-start(bf16[6,64,512]{2,1,0:T(8,128)(2,1)} %fusion.91) | copy-start | bytes 1179652
  648.4 5.8 copy-start.40
  648.4 5.8 copy-start.55
  648.4 277.2 %reduce-scatter.7.cloned.1.call-start = ((), (), s32[]{:S(2)}) async-start(), calls=%async_computation.6 | async-start | bytes 7077888
  648.6 7.8 copy-start.17
  656.4 5.4 copy-start.27
  656.4 5.4 copy-start.29
  656.4 5.4 copy-start.34
  656.4 5.4 copy-start.66
  671.7 100.3 %copy-start.57 = (bf16[1536,6]{0,1:T(8,128)(2,1)S(1)}, bf16[1536,6]{0,1:T(8,128)(2,1)}, u32[]{:S(2)}) copy-start(bf16[1536,6]{0,1:T(8,128)(2,1)} %convolution_convert_fusion.6) | copy-start | bytes 55300
  671.7 100.3 %copy-start.58 = (bf16[1536,1]{0,1:T(2,128)(2,1)S(1)}, bf16[1536,1]{0,1:T(2,128)(2,1)}, u32[]{:S(2)}) copy-start(bf16[1536,1]{0,1:T(2,128)(2,1)} %fusion.111) | copy-start | bytes 9220
  807.4 6.5 copy-start.42
  807.4 6.5 copy-start.53
  807.4 288.5 %reduce-scatter.5.cloned.1.call-start = ((), (), s32[]{:S(2)}) async-start(), calls=%async_computation.5 | async-start | bytes 11059200 | tf_op jit(solution)/shard_map/reduce_scatter | solution.py:246
  807.7 6.2 copy-start.6
  807.7 6.2 copy-start.68
  807.7 6.2 copy-start.70
  813.9 7.9 copy-start.59
  (23 other events, 59.9 us)
Sparse Core Ops, SparseCore 0:
  292.3 68.6 all-reduce.4
  469.5 66.5 all-reduce.6
  648.5 119.6 all-reduce.8
Sparse Core Ops, SparseCore 1:
  295.4 142.1 all-gather.1
  807.5 118.1 reduce-scatter.6
  929.1 166.8 reduce-scatter.4
